TPU v7x, 768 devices: a whole 4x8x12 slice. The times are simulated.
768 devices in a mesh: row: 16 (over y, core), col: 48 (over z, x).
Axes of the slice: x: 4, y: 8, z: 12, core: 2. Of those that a mesh axis runs over, the one named last changes fastest.
Arguments:
- matrix: float32 [4, 16, 48, 256, 256], P(None, 'row', 'col'), as said below
- present: int32 [4, 16, 48], P(None, 'row', 'col'), may hold values from 0 to 1, as said below
- update: int32 [2, 4, 16, 48], P(None, None, 'row', 'col'), may hold values from 0 to 1, as said below
Outputs:
- factored: float32 [4, 16, 48, 256, 256], P(None, 'row', 'col')
Inputs may be any that keep to these rules, and one draw needn't show every extreme that they name: `present`: listed tiles lie on or below the diagonal (row >= column). Tiles (0, 0), (1, 0), (1, 1) and every diagonal tile (c, c) of the window, that is with c < 64 and c < 48, are listed; in column 1 every row i >= 1 whose tile in column 0 is listed is listed too. update[k, s, r, c] is 1 exactly where c > k and the tiles (i, c), (i, k) and (c, k) are all listed, with i = r + 16 s. `matrix`: unlisted tiles are zero. Tile (0, 0) is symmetric positive definite, and so is tile (1, 1) minus P0(1) P0(1)^T.
All inputs are finite; a program needn't handle non-finite values.
Results may differ from a plain program's by a relative error of at most 0.0001.
Values sent between devices are 32-bit elements; how exact they have to be, the bound alone decides.
No kernel may reach another device: no remote copies, remote signals or barrier semaphores. Data moves between devices by JAX's collectives and lax.ppermute only.
A program may use at most 32 MiB of HBM per device.

v0:
```python
import numpy as np
import jax
import jax.numpy as jnp
from jax import lax
from jax.sharding import Mesh
from jax.sharding import PartitionSpec as P

AXES = ("y", "core", "z", "x")
ROW = ("y", "core")
COL = ("z", "x")


def split_rounds(n, fan=2):
    spans = [(0, n)]
    rounds = []
    while any(length > 1 for _, length in spans):
        sends = [[] for _ in range(fan)]
        next_spans = []
        for start, length in spans:
            parts = min(fan + 1, length)
            sizes = [length // parts + (1 if i < length % parts else 0) for i in range(parts)]
            offset = start
            for i, size in enumerate(sizes):
                if i > 0:
                    sends[i - 1].append((start, offset))
                next_spans.append((offset, size))
                offset += size
        rounds.append([s for s in sends if s])
        spans = next_spans
    return rounds


class Grid:
    def __init__(self, shape):
        self.shape = shape
        ny, nk, nz, nx = shape
        self.n_row = ny * nk
        self.n_col = nz * nx
        self.y = lax.axis_index("y")
        self.core = lax.axis_index("core")
        self.z = lax.axis_index("z")
        self.x = lax.axis_index("x")
        self.row = self.y * nk + self.core
        self.col = self.z * nx + self.x
        self.lin = ((self.y * nk + self.core) * nz + self.z) * nx + self.x

    def index(self, y, k, z, x):
        ny, nk, nz, nx = self.shape
        return ((y * nk + k) * nz + z) * nx + x

    def send(self, value, pairs):
        perm = [(self.index(*s), self.index(*d)) for s, d in pairs]
        got = lax.ppermute(value, AXES, perm)
        mask = np.zeros(int(np.prod(self.shape)), bool)
        mask[[d for _, d in perm]] = True
        hit = jnp.asarray(mask)[self.lin]
        return got, hit

    def down_columns(self, value, roots):
        ny, nk, nz, nx = self.shape
        pairs = []
        for c, r in roots.items():
            z, x = divmod(c, nx)
            y0, k0 = divmod(r, nk)
            for k in range(nk):
                if k != k0:
                    pairs.append(((y0, k0, z, x), (y0, k, z, x)))
        if pairs:
            got, hit = self.send(value, pairs)
            value = jnp.where(hit, got, value)
        for sends in split_rounds(ny):
            results = []
            for offsets in sends:
                pairs = []
                for c, r in roots.items():
                    z, x = divmod(c, nx)
                    y0 = r // nk
                    for a, b in offsets:
                        for k in range(nk):
                            pairs.append((((y0 + a) % ny, k, z, x), ((y0 + b) % ny, k, z, x)))
                results.append(self.send(value, pairs))
            for got, hit in results:
                value = jnp.where(hit, got, value)
        return value

    def along_rows(self, tiles, root_col, skip=()):
        ny, nk, nz, nx = self.shape
        slots = tiles.shape[0]
        assert slots == nx
        z0, x0 = divmod(root_col, nx)
        skipped = {divmod(c, nx) for c in skip}
        rows = [(y, k) for y in range(ny) for k in range(nk)]
        line_root = {x0: z0}
        held = tiles[0]
        for j in range(1, nx):
            x = (x0 + j) % nx
            z = z0
            while (z, x) in skipped:
                z = (z + 1) % nz
            line_root[x] = z
            pairs = [((y, k, z0, x0), (y, k, z, x)) for y, k in rows]
            got, hit = self.send(tiles[j], pairs)
            held = jnp.where(hit, got, held)
        trees = {}
        for x in range(nx):
            zs = [(line_root[x] + t) % nz for t in range(nz)]
            trees[x] = [z for z in zs if (z, x) not in skipped]
        depth = max(len(split_rounds(len(t))) for t in trees.values())
        plans = {x: split_rounds(len(t)) for x, t in trees.items()}
        for level in range(depth):
            fan = max(len(plans[x][level]) for x in plans if level < len(plans[x]))
            results = []
            for i in range(fan):
                pairs = []
                for x, plan in plans.items():
                    if level < len(plan) and i < len(plan[level]):
                        zs = trees[x]
                        for a, b in plan[level][i]:
                            pairs += [((y, k, zs[a], x), (y, k, zs[b], x)) for y, k in rows]
                if pairs:
                    results.append(self.send(held, pairs))
            for got, hit in results:
                held = jnp.where(hit, got, held)
        buffers = [held]
        table = np.zeros((int(np.prod(self.shape)), nx), np.int32)
        for d in range(1, nx):
            pairs = []
            for z in range(nz):
                for x in range(nx):
                    t = (x + d) % nx
                    if (z, x) in skipped or (z, t) in skipped or (z, t) == (z0, x0):
                        continue
                    pairs += [((y, k, z, x), (y, k, z, t)) for y, k in rows]
            if pairs:
                got, _ = self.send(held, pairs)
                buffers.append(got)
                for y, k in rows:
                    for z in range(nz):
                        for t in range(nx):
                            x = (t - d) % nx
                            if (z, x) not in skipped and (z, t) not in skipped:
                                table[self.index(y, k, z, t), (x - x0) % nx] = len(buffers) - 1
        for z, x in sorted(skipped):
            j = (x - x0) % nx
            for t in range(nx):
                if (z, t) in skipped or (z, t) == (z0, x0):
                    continue
                pairs = [((y, k, z0, x0), (y, k, z, t)) for y, k in rows]
                got, _ = self.send(tiles[j], pairs)
                buffers.append(got)
                for y, k in rows:
                    table[self.index(y, k, z, t), j] = len(buffers) - 1
        for y, k in rows:
            for z in range(nz):
                for x in range(nx):
                    table[self.index(y, k, z, x), (x - x0) % nx] = 0
        order = jnp.asarray(table)[self.lin]
        out = jnp.take(jnp.stack(buffers), order, axis=0)
        is_root = (self.z == z0) & (self.x == x0)
        return jnp.where(is_root, tiles, out)


def solve_panel(factor, blocks):
    count = blocks.shape[0]
    width = blocks.shape[-1]
    stacked = jnp.transpose(blocks, (2, 0, 1)).reshape(width, count * width)
    solved = jax.scipy.linalg.solve_triangular(factor, stacked, lower=True)
    return jnp.transpose(solved.reshape(width, count, width), (1, 2, 0))


def products(rows, far):
    return jnp.einsum("sab,db->sad", rows, far, precision=lax.Precision.HIGHEST)


def make_on_device(shape):
    def on_device(matrix, present, update):
        g = Grid(shape)
        tiles = matrix[:, 0, 0]
        listed = present[:, 0, 0].astype(jnp.float32)
        flags = update[:, :, 0, 0].astype(jnp.float32)
        width = tiles.shape[-1]
        n_row, n_col = g.n_row, g.n_col
        identity = jnp.eye(width, dtype=jnp.float32)
        far_slot = g.col // n_row
        far_root = {c: c % n_row for c in range(2, n_col)}

        def factor_on_owner(k, tile):
            owner = (g.row == k) & (g.col == k)
            factor = lax.cond(owner, jnp.linalg.cholesky, lambda t: identity, tile)
            return owner, g.down_columns(factor, {k: k})

        def solve_column(k, owner, factor, work):
            solved = lax.cond(g.col == k, lambda d: solve_panel(factor, d), lambda d: d, work)
            return solved.at[0].set(jnp.where(owner, factor, solved[0]))

        owner0, factor0 = factor_on_owner(0, tiles[0])
        p0 = solve_column(0, owner0, factor0, tiles)
        got, _ = g.send(p0[0], [((0, 1, 0, 0), (0, 1, 0, 1))])
        work11 = tiles[0] - flags[0, 0] * products(got[None], got)[0]
        f01 = g.down_columns(p0[0], {0: 1 % n_row})
        pairs = [((y, k, 0, 0), (y, k, 0, 1)) for y in range(shape[0]) for k in range(shape[1])]
        q01, _ = g.send(products(p0, f01), pairs)
        owner1, factor1 = factor_on_owner(1, work11)
        work1 = tiles - flags[0][:, None, None] * q01
        p1 = solve_column(1, owner1, factor1, work1)

        r0 = g.along_rows(p0, 0, skip=(1,))
        f0 = g.down_columns(lax.dynamic_index_in_dim(r0, far_slot, 0, keepdims=False), far_root)
        r1 = g.along_rows(p1, 1, skip=(0,))
        f1 = g.down_columns(lax.dynamic_index_in_dim(r1, far_slot, 0, keepdims=False), far_root)
        rest = (tiles - flags[0][:, None, None] * products(r0, f0)) - flags[1][:, None, None] * products(r1, f1)
        out = jnp.where(g.col == 0, p0, jnp.where(g.col == 1, p1, rest))
        return (out * listed[:, None, None])[:, None, None]

    return on_device


def solution(mesh):
    n_row = mesh.shape["row"]
    n_col = mesh.shape["col"]
    shape = (n_row // 2, 2, n_col // 4, 4)
    finer = Mesh(mesh.devices.reshape(shape), AXES)
    return jax.shard_map(
        make_on_device(shape),
        mesh=finer,
        in_specs=(P(None, ROW, COL, None, None), P(None, ROW, COL), P(None, None, ROW, COL)),
        out_specs=P(None, ROW, COL, None, None),
        check_vma=False,
    )
```

profile of v0, /device:TPU:4, one launch (start us, length us, event | category | flops | bytes accessed | tf_op | source)
XLA Modules:
  0.0 505.8 jit_solution(2551583754982848415)
XLA Ops:
  13.5 3.0 conditional.5
  14.0 1.3 copy.65
  16.6 1.6 copy.56
  25.8 91.4 %collective-permute-done.18 = f32[256,256]{1,0:T(8,128)S(1)} collective-permute-done((f32[256,256]{1,0:T(8,128)S(1)}, f32[256,256]{1,0:T(8,128)S(1)}, u32[]{:S(2)}, u32[]{:S(2)}) %collective-permute-start.18) | collective-permute-done | bytes 262176 | tf_op jit(solution)/shard_map/ppermute | solution.py:53
  117.2 2.6 select_select_fusion.11
  119.7 1.4 collective-permute-start.6
  121.1 1.4 collective-permute-start.7
  123.8 1.3 select_select_fusion.14
  128.5 1.6 broadcast_select_fusion.5
  131.9 3.2 fusion.26
  135.1 1.6 collective-permute-start.10
  139.4 1.4 select_select_fusion.13
  141.5 1.4 collective-permute-start.16
  146.0 1.9 select_select_fusion.10
  148.0 2.0 collective-permute-start.22
  149.9 2.0 collective-permute-start.23
  153.3 1.4 multiply_subtract_fusion.1
  154.7 4.4 conditional.7
  154.7 1.3 copy.68
  159.1 1.6 copy.61
  166.5 2.2 select_select_fusion.9
  170.1 78.9 %collective-permute-done.37 = f32[256,256]{1,0:T(8,128)S(1)} collective-permute-done((f32[256,256]{1,0:T(8,128)S(1)}, f32[256,256]{1,0:T(8,128)S(1)}, u32[]{:S(2)}, u32[]{:S(2)}) %collective-permute-start.37) | collective-permute-done | bytes 262176 | tf_op jit(solution)/shard_map/ppermute | solution.py:53
  249.0 2.9 select_select_fusion.7
  257.2 1.5 bitcast_dynamic-update-slice_fusion.13
  258.7 6.7 %collective-permute-start.25 = (f32[256,256]{1,0:T(8,128)}, f32[256,256]{1,0:T(8,128)}, u32[]{:S(2)}, u32[]{:S(2)}) collective-permute-start(f32[256,256]{1,0:T(8,128)} %get-tuple-element.162), channel_id=1, source_target_pairs={{2,3},{50,51},{98,99},{146,147},{194,195},{242,243},{290,291},{338... | collective-permute-start | bytes 786440 | tf_op jit(solution)/shard_map/ppermute | solution.py:53
  266.6 20.5 %collective-permute-start.40 = (f32[256,256]{1,0:T(8,128)S(1)}, f32[256,256]{1,0:T(8,128)}, u32[]{:S(2)}, u32[]{:S(2)}) collective-permute-start(f32[256,256]{1,0:T(8,128)S(1)} %select_select_fusion.6), channel_id=1, source_target_pairs={{4,16},{52,64},{100,112},{148,160},{196,208},{244,256},{292,304},{... | collective-permute-start | bytes 786440 | tf_op jit(solution)/shard_map/ppermute | solution.py:53
  287.1 5.3 %collective-permute-start.41 = (f32[256,256]{1,0:T(8,128)S(1)}, f32[256,256]{1,0:T(8,128)}, u32[]{:S(2)}, u32[]{:S(2)}) collective-permute-start(f32[256,256]{1,0:T(8,128)S(1)} %select_select_fusion.6), channel_id=1, source_target_pairs={{4,12},{52,60},{100,108},{148,156},{196,204},{244,252},{292,300},{... | collective-permute-start | bytes 786440 | tf_op jit(solution)/shard_map/ppermute | solution.py:53
  296.9 16.0 %collective-permute-start.26 = (f32[256,256]{1,0:T(8,128)}, f32[256,256]{1,0:T(8,128)S(1)}, u32[]{:S(2)}, u32[]{:S(2)}) collective-permute-start(f32[256,256]{1,0:T(8,128)} %get-tuple-element.162), channel_id=1, source_target_pairs={{0,2},{48,50},{96,98},{144,146},{192,194},{240,242},{288,290},{336... | collective-permute-start | bytes 786440 | tf_op jit(solution)/shard_map/ppermute | solution.py:53
  312.8 1.7 bitcast_dynamic-update-slice_fusion.12
  314.5 20.5 %collective-permute-start.27 = (f32[256,256]{1,0:T(8,128)}, f32[256,256]{1,0:T(8,128)S(1)}, u32[]{:S(2)}, u32[]{:S(2)}) collective-permute-start(f32[256,256]{1,0:T(8,128)} %get-tuple-element.162), channel_id=1, source_target_pairs={{0,3},{48,51},{96,99},{144,147},{192,195},{240,243},{288,291},{336... | collective-permute-start | bytes 786440 | tf_op jit(solution)/shard_map/ppermute | solution.py:53
  335.0 1.4 select_select_fusion.5
  336.4 4.5 collective-permute-start.42
  341.6 2.0 collective-permute-done.27
  344.3 2.4 collective-permute-done.42
  346.7 1.4 bitcast_dynamic-update-slice_fusion.7
  348.1 19.1 %collective-permute-start.43 = (f32[256,256]{1,0:T(8,128)}, f32[256,256]{1,0:T(8,128)S(1)}, u32[]{:S(2)}, u32[]{:S(2)}) collective-permute-start(f32[256,256]{1,0:T(8,128)} %get-tuple-element.166), channel_id=1, source_target_pairs={{1,2},{49,50},{97,98},{145,146},{193,194},{241,242},{289,290},{337... | collective-permute-start | bytes 786440 | tf_op jit(solution)/shard_map/ppermute | solution.py:53
  368.0 20.5 %collective-permute-start.44 = (f32[256,256]{1,0:T(8,128)}, f32[256,256]{1,0:T(8,128)}, u32[]{:S(2)}, u32[]{:S(2)}) collective-permute-start(f32[256,256]{1,0:T(8,128)} %get-tuple-element.166), channel_id=1, source_target_pairs={{1,3},{49,51},{97,99},{145,147},{193,195},{241,243},{289,291},{337... | collective-permute-start | bytes 786440 | tf_op jit(solution)/shard_map/ppermute | solution.py:53
  389.2 3.1 gather_fusion
  394.3 19.2 %collective-permute-start.45 = (f32[256,256]{1,0:T(8,128)}, f32[256,256]{1,0:T(8,128)S(1)}, u32[]{:S(2)}, u32[]{:S(2)}) collective-permute-start(f32[256,256]{1,0:T(8,128)} %get-tuple-element.166), channel_id=1, source_target_pairs={{3,2},{51,50},{99,98},{147,146},{195,194},{243,242},{291,290},{339... | collective-permute-start | bytes 786440 | tf_op jit(solution)/shard_map/ppermute | solution.py:53
  414.2 1.7 bitcast_dynamic-update-slice_fusion.5
  415.8 6.2 %collective-permute-done.45 = f32[256,256]{1,0:T(8,128)S(1)} collective-permute-done((f32[256,256]{1,0:T(8,128)}, f32[256,256]{1,0:T(8,128)S(1)}, u32[]{:S(2)}, u32[]{:S(2)}) %collective-permute-start.45) | collective-permute-done | bytes 262176 | tf_op jit(solution)/shard_map/ppermute | solution.py:53
  424.2 3.0 gather_fusion.1
  427.2 1.5 select_select_fusion.2
  437.8 29.0 %collective-permute-start.52 = (f32[256,256]{1,0:T(8,128)S(1)}, f32[256,256]{1,0:T(8,128)S(1)}, u32[]{:S(2)}, u32[]{:S(2)}) collective-permute-start(f32[256,256]{1,0:T(8,128)S(1)} %select_select_fusion.4), channel_id=1, source_target_pairs={{98,194},{146,242},{386,482},{434,530},{674,2},{722,50},{99,195},{... | collective-permute-start | bytes 786440 | tf_op jit(solution)/shard_map/ppermute | solution.py:53
  469.9 21.7 %collective-permute-start.34 = (f32[256,256]{1,0:T(8,128)S(1)}, f32[256,256]{1,0:T(8,128)S(1)}, u32[]{:S(2)}, u32[]{:S(2)}) collective-permute-start(f32[256,256]{1,0:T(8,128)S(1)} %select_select_fusion.8), channel_id=1, source_target_pairs={{98,194},{146,242},{386,482},{434,530},{674,2},{722,50},{99,195},{... | collective-permute-start | bytes 786440 | tf_op jit(solution)/shard_map/ppermute | solution.py:53
  491.6 2.3 convolution_multiply_fusion
  494.0 7.9 %collective-permute-done.34 = f32[256,256]{1,0:T(8,128)S(1)} collective-permute-done((f32[256,256]{1,0:T(8,128)S(1)}, f32[256,256]{1,0:T(8,128)S(1)}, u32[]{:S(2)}, u32[]{:S(2)}) %collective-permute-start.34) | collective-permute-done | bytes 262176 | tf_op jit(solution)/shard_map/ppermute | solution.py:53
  501.9 3.5 fusion.23
  (233 shorter events, 77.9 us)
Async XLA Ops:
  5.0 2.6 collective-permute-start.1
  19.3 6.5 %collective-permute-start.17 = (f32[256,256]{1,0:T(8,128)S(1)}, f32[256,256]{1,0:T(8,128)S(1)}, u32[]{:S(2)}, u32[]{:S(2)}) collective-permute-start(f32[256,256]{1,0:T(8,128)S(1)} %get-tuple-element.191), channel_id=1, source_target_pairs={{0,3},{48,51},{96,99},{144,147},{192,195},{240,243},{288,291},{336... | collective-permute-start | bytes 786440 | tf_op jit(solution)/shard_map/ppermute | solution.py:53
  20.0 97.1 %collective-permute-start.18 = (f32[256,256]{1,0:T(8,128)S(1)}, f32[256,256]{1,0:T(8,128)S(1)}, u32[]{:S(2)}, u32[]{:S(2)}) collective-permute-start(f32[256,256]{1,0:T(8,128)S(1)} %get-tuple-element.190), channel_id=1, source_target_pairs={{0,2},{48,50},{96,98},{144,146},{192,194},{240,242},{288,290},{336... | collective-permute-start | bytes 786440 | tf_op jit(solution)/shard_map/ppermute | solution.py:53
  21.3 95.8 %collective-permute-start.19 = (f32[256,256]{1,0:T(8,128)S(1)}, f32[256,256]{1,0:T(8,128)S(1)}, u32[]{:S(2)}, u32[]{:S(2)}) collective-permute-start(f32[256,256]{1,0:T(8,128)S(1)} %get-tuple-element.189), channel_id=1, source_target_pairs={{0,5},{48,53},{96,101},{144,149},{192,197},{240,245},{288,293},{33... | collective-permute-start | bytes 786440 | tf_op jit(solution)/shard_map/ppermute | solution.py:53
  22.0 95.2 %collective-permute-start.5 = (f32[256,256]{1,0:T(8,128)S(1)}, f32[256,256]{1,0:T(8,128)S(1)}, u32[]{:S(2)}, u32[]{:S(2)}) collective-permute-start(f32[256,256]{1,0:T(8,128)S(1)} %get-tuple-element.168), channel_id=1, source_target_pairs={{48,0}} | collective-permute-start | bytes 786440 | tf_op jit(solution)/shard_map/ppermute | solution.py:53
  25.1 97.4 %collective-permute-start.11 = (f32[256,256]{1,0:T(8,128)S(1)}, f32[256,256]{1,0:T(8,128)S(1)}, u32[]{:S(2)}, u32[]{:S(2)}) collective-permute-start(f32[256,256]{1,0:T(8,128)S(1)} %get-tuple-element.168), channel_id=1, source_target_pairs={{48,49}} | collective-permute-start | bytes 786440 | tf_op jit(solution)/shard_map/ppermute | solution.py:53
  119.7 4.1 collective-permute-start.6
  121.1 2.7 collective-permute-start.7
  123.1 5.3 %collective-permute-start.12 = (f32[256,256]{1,0:T(8,128)}, f32[256,256]{1,0:T(8,128)S(1)}, u32[]{:S(2)}, u32[]{:S(2)}) collective-permute-start(f32[256,256]{1,0:T(8,128)} %get-tuple-element.296), channel_id=1, source_target_pairs={{49,1}} | collective-permute-start | bytes 786440 | tf_op jit(solution)/shard_map/ppermute | solution.py:53
  125.2 6.7 %collective-permute-start.8 = (f32[256,256]{1,0:T(8,128)S(1)}, f32[256,256]{1,0:T(8,128)S(1)}, u32[]{:S(2)}, u32[]{:S(2)}) collective-permute-start(f32[256,256]{1,0:T(8,128)S(1)} %select_select_fusion.14), channel_id=1, source_target_pairs={{0,192},{48,240},{288,480},{336,528}} | collective-permute-start | bytes 786440 | tf_op jit(solution)/shard_map/ppermute | solution.py:53
  125.8 6.0 %collective-permute-start.9 = (f32[256,256]{1,0:T(8,128)S(1)}, f32[256,256]{1,0:T(8,128)S(1)}, u32[]{:S(2)}, u32[]{:S(2)}) collective-permute-start(f32[256,256]{1,0:T(8,128)S(1)} %select_select_fusion.14), channel_id=1, source_target_pairs={{0,96},{48,144},{288,384},{336,432},{576,672},{624,720}} | collective-permute-start | bytes 786440 | tf_op jit(solution)/shard_map/ppermute | solution.py:53
  130.2 9.2 %collective-permute-start.13 = (f32[256,256]{1,0:T(8,128)S(1)}, f32[256,256]{1,0:T(8,128)S(1)}, u32[]{:S(2)}, u32[]{:S(2)}) collective-permute-start(f32[256,256]{1,0:T(8,128)S(1)} %broadcast_select_fusion.5), channel_id=1, source_target_pairs={{1,577},{49,625}} | collective-permute-start | bytes 786440 | tf_op jit(solution)/shard_map/ppermute | solution.py:53
  131.0 8.4 %collective-permute-start.14 = (f32[256,256]{1,0:T(8,128)S(1)}, f32[256,256]{1,0:T(8,128)S(1)}, u32[]{:S(2)}, u32[]{:S(2)}) collective-permute-start(f32[256,256]{1,0:T(8,128)S(1)} %broadcast_select_fusion.5), channel_id=1, source_target_pairs={{1,289},{49,337}} | collective-permute-start | bytes 786440 | tf_op jit(solution)/shard_map/ppermute | solution.py:53
  135.1 18.1 %collective-permute-start.10 = (f32[4,256,256]{2,1,0:T(8,128)}, f32[4,256,256]{2,1,0:T(8,128)}, u32[]{:S(2)}, u32[]{:S(2)}) collective-permute-start(f32[4,256,256]{2,1,0:T(8,128)} %fusion.26), channel_id=1, source_target_pairs={{0,1},{48,49},{96,97},{144,145},{192,193},{240,241},{288,289},{336... | collective-permute-start | bytes 3145736 | tf_op jit(solution)/shard_map/ppermute | solution.py:53
  136.8 9.3 %collective-permute-start.20 = (f32[256,256]{1,0:T(8,128)S(1)}, f32[256,256]{1,0:T(8,128)S(1)}, u32[]{:S(2)}, u32[]{:S(2)}) collective-permute-start(f32[256,256]{1,0:T(8,128)S(1)} %get-tuple-element.195), channel_id=1, source_target_pairs={{0,32},{48,80},{96,128},{144,176},{192,224},{240,272},{288,320},{3... | collective-permute-start | bytes 786440 | tf_op jit(solution)/shard_map/ppermute | solution.py:53
  138.1 8.0 %collective-permute-start.21 = (f32[256,256]{1,0:T(8,128)S(1)}, f32[256,256]{1,0:T(8,128)S(1)}, u32[]{:S(2)}, u32[]{:S(2)}) collective-permute-start(f32[256,256]{1,0:T(8,128)S(1)} %get-tuple-element.195), channel_id=1, source_target_pairs={{0,16},{48,64},{96,112},{144,160},{192,208},{240,256},{288,304},{3... | collective-permute-start | bytes 786440 | tf_op jit(solution)/shard_map/ppermute | solution.py:53
  140.8 11.1 %collective-permute-start.15 = (f32[256,256]{1,0:T(8,128)S(1)}, f32[256,256]{1,0:T(8,128)S(1)}, u32[]{:S(2)}, u32[]{:S(2)}) collective-permute-start(f32[256,256]{1,0:T(8,128)S(1)} %select_select_fusion.13), channel_id=1, source_target_pairs={{1,193},{49,241},{289,481},{337,529}} | collective-permute-start | bytes 786440 | tf_op jit(solution)/shard_map/ppermute | solution.py:53
  141.5 10.4 %collective-permute-start.16 = (f32[256,256]{1,0:T(8,128)S(1)}, f32[256,256]{1,0:T(8,128)}, u32[]{:S(2)}, u32[]{:S(2)}) collective-permute-start(f32[256,256]{1,0:T(8,128)S(1)} %select_select_fusion.13), channel_id=1, source_target_pairs={{1,97},{49,145},{289,385},{337,433},{577,673},{625,721}} | collective-permute-start | bytes 786440 | tf_op jit(solution)/shard_map/ppermute | solution.py:53
  148.0 18.5 %collective-permute-start.22 = (f32[256,256]{1,0:T(8,128)}, f32[256,256]{1,0:T(8,128)}, u32[]{:S(2)}, u32[]{:S(2)}) collective-permute-start(f32[256,256]{1,0:T(8,128)} %select_select_fusion.10), channel_id=1, source_target_pairs={{0,12},{48,60},{96,108},{144,156},{192,204},{240,252},{288,300},{3... | collective-permute-start | bytes 786440 | tf_op jit(solution)/shard_map/ppermute | solution.py:53
  149.9 16.6 %collective-permute-start.23 = (f32[256,256]{1,0:T(8,128)}, f32[256,256]{1,0:T(8,128)}, u32[]{:S(2)}, u32[]{:S(2)}) collective-permute-start(f32[256,256]{1,0:T(8,128)} %select_select_fusion.10), channel_id=1, source_target_pairs={{0,8},{48,56},{96,104},{144,152},{192,200},{240,248},{288,296},{33... | collective-permute-start | bytes 786440 | tf_op jit(solution)/shard_map/ppermute | solution.py:53
  161.8 8.2 %collective-permute-start.35 = (f32[256,256]{1,0:T(8,128)S(1)}, f32[256,256]{1,0:T(8,128)S(1)}, u32[]{:S(2)}, u32[]{:S(2)}) collective-permute-start(f32[256,256]{1,0:T(8,128)S(1)} %get-tuple-element.194), channel_id=1, source_target_pairs={{1,4},{49,52},{97,100},{145,148},{193,196},{241,244},{289,292},{33... | collective-permute-start | bytes 786440 | tf_op jit(solution)/shard_map/ppermute | solution.py:53
  162.7 7.4 %collective-permute-start.36 = (f32[256,256]{1,0:T(8,128)S(1)}, f32[256,256]{1,0:T(8,128)S(1)}, u32[]{:S(2)}, u32[]{:S(2)}) collective-permute-start(f32[256,256]{1,0:T(8,128)S(1)} %get-tuple-element.193), channel_id=1, source_target_pairs={{1,3},{49,51},{97,99},{145,147},{193,195},{241,243},{289,291},{337... | collective-permute-start | bytes 786440 | tf_op jit(solution)/shard_map/ppermute | solution.py:53
  163.3 85.6 %collective-permute-start.37 = (f32[256,256]{1,0:T(8,128)S(1)}, f32[256,256]{1,0:T(8,128)S(1)}, u32[]{:S(2)}, u32[]{:S(2)}) collective-permute-start(f32[256,256]{1,0:T(8,128)S(1)} %get-tuple-element.192), channel_id=1, source_target_pairs={{1,2},{49,50},{97,98},{145,146},{193,194},{241,242},{289,290},{337... | collective-permute-start | bytes 786440 | tf_op jit(solution)/shard_map/ppermute | solution.py:53
  168.7 88.4 %collective-permute-start.24 = (f32[256,256]{1,0:T(8,128)S(1)}, f32[256,256]{1,0:T(8,128)S(1)}, u32[]{:S(2)}, u32[]{:S(2)}) collective-permute-start(f32[256,256]{1,0:T(8,128)S(1)} %select_select_fusion.9), channel_id=1, source_target_pairs={{0,4},{48,52},{96,100},{144,148},{192,196},{240,244},{288,292},{33... | collective-permute-start | bytes 786440 | tf_op jit(solution)/shard_map/ppermute | solution.py:53
  251.9 13.4 %collective-permute-start.38 = (f32[256,256]{1,0:T(8,128)S(1)}, f32[256,256]{1,0:T(8,128)S(1)}, u32[]{:S(2)}, u32[]{:S(2)}) collective-permute-start(f32[256,256]{1,0:T(8,128)S(1)} %select_select_fusion.7), channel_id=1, source_target_pairs={{4,36},{52,84},{100,132},{148,180},{196,228},{244,276},{292,324},{... | collective-permute-start | bytes 786440 | tf_op jit(solution)/shard_map/ppermute | solution.py:53
  253.2 12.1 %collective-permute-start.39 = (f32[256,256]{1,0:T(8,128)S(1)}, f32[256,256]{1,0:T(8,128)S(1)}, u32[]{:S(2)}, u32[]{:S(2)}) collective-permute-start(f32[256,256]{1,0:T(8,128)S(1)} %select_select_fusion.7), channel_id=1, source_target_pairs={{4,20},{52,68},{100,116},{148,164},{196,212},{244,260},{292,308},{... | collective-permute-start | bytes 786440 | tf_op jit(solution)/shard_map/ppermute | solution.py:53
  258.7 38.2 %collective-permute-start.25 = (f32[256,256]{1,0:T(8,128)}, f32[256,256]{1,0:T(8,128)}, u32[]{:S(2)}, u32[]{:S(2)}) collective-permute-start(f32[256,256]{1,0:T(8,128)} %get-tuple-element.162), channel_id=1, source_target_pairs={{2,3},{50,51},{98,99},{146,147},{194,195},{242,243},{290,291},{338... | collective-permute-start | bytes 786440 | tf_op jit(solution)/shard_map/ppermute | solution.py:53
  266.6 47.9 %collective-permute-start.40 = (f32[256,256]{1,0:T(8,128)S(1)}, f32[256,256]{1,0:T(8,128)}, u32[]{:S(2)}, u32[]{:S(2)}) collective-permute-start(f32[256,256]{1,0:T(8,128)S(1)} %select_select_fusion.6), channel_id=1, source_target_pairs={{4,16},{52,64},{100,112},{148,160},{196,208},{244,256},{292,304},{... | collective-permute-start | bytes 786440 | tf_op jit(solution)/shard_map/ppermute | solution.py:53
  287.1 47.9 %collective-permute-start.41 = (f32[256,256]{1,0:T(8,128)S(1)}, f32[256,256]{1,0:T(8,128)}, u32[]{:S(2)}, u32[]{:S(2)}) collective-permute-start(f32[256,256]{1,0:T(8,128)S(1)} %select_select_fusion.6), channel_id=1, source_target_pairs={{4,12},{52,60},{100,108},{148,156},{196,204},{244,252},{292,300},{... | collective-permute-start | bytes 786440 | tf_op jit(solution)/shard_map/ppermute | solution.py:53
  294.9 72.3 %collective-permute-start.28 = (f32[256,256]{1,0:T(8,128)}, f32[256,256]{1,0:T(8,128)S(1)}, u32[]{:S(2)}, u32[]{:S(2)}) collective-permute-start(f32[256,256]{1,0:T(8,128)} %copy-done.5), channel_id=1, source_target_pairs={{0,2},{48,50},{96,98},{144,146},{192,194},{240,242},{288,290},{336... | collective-permute-start | bytes 786440 | tf_op jit(solution)/shard_map/ppermute | solution.py:53
  296.2 92.3 %collective-permute-start.29 = (f32[256,256]{1,0:T(8,128)}, f32[256,256]{1,0:T(8,128)S(1)}, u32[]{:S(2)}, u32[]{:S(2)}) collective-permute-start(f32[256,256]{1,0:T(8,128)} %copy-done.5), channel_id=1, source_target_pairs={{0,3},{48,51},{96,99},{144,147},{192,195},{240,243},{288,291},{336... | collective-permute-start | bytes 786440 | tf_op jit(solution)/shard_map/ppermute | solution.py:53
  296.9 44.0 %collective-permute-start.26 = (f32[256,256]{1,0:T(8,128)}, f32[256,256]{1,0:T(8,128)S(1)}, u32[]{:S(2)}, u32[]{:S(2)}) collective-permute-start(f32[256,256]{1,0:T(8,128)} %get-tuple-element.162), channel_id=1, source_target_pairs={{0,2},{48,50},{96,98},{144,146},{192,194},{240,242},{288,290},{336... | collective-permute-start | bytes 786440 | tf_op jit(solution)/shard_map/ppermute | solution.py:53
  314.5 29.1 %collective-permute-start.27 = (f32[256,256]{1,0:T(8,128)}, f32[256,256]{1,0:T(8,128)S(1)}, u32[]{:S(2)}, u32[]{:S(2)}) collective-permute-start(f32[256,256]{1,0:T(8,128)} %get-tuple-element.162), channel_id=1, source_target_pairs={{0,3},{48,51},{96,99},{144,147},{192,195},{240,243},{288,291},{336... | collective-permute-start | bytes 786440 | tf_op jit(solution)/shard_map/ppermute | solution.py:53
  336.4 10.3 %collective-permute-start.42 = (f32[256,256]{1,0:T(8,128)S(1)}, f32[256,256]{1,0:T(8,128)S(1)}, u32[]{:S(2)}, u32[]{:S(2)}) collective-permute-start(f32[256,256]{1,0:T(8,128)S(1)} %select_select_fusion.5), channel_id=1, source_target_pairs={{4,8},{52,56},{100,104},{148,152},{196,200},{244,248},{292,296},{3... | collective-permute-start | bytes 786440 | tf_op jit(solution)/shard_map/ppermute | solution.py:53
  348.1 65.3 %collective-permute-start.43 = (f32[256,256]{1,0:T(8,128)}, f32[256,256]{1,0:T(8,128)S(1)}, u32[]{:S(2)}, u32[]{:S(2)}) collective-permute-start(f32[256,256]{1,0:T(8,128)} %get-tuple-element.166), channel_id=1, source_target_pairs={{1,2},{49,50},{97,98},{145,146},{193,194},{241,242},{289,290},{337... | collective-permute-start | bytes 786440 | tf_op jit(solution)/shard_map/ppermute | solution.py:53
  368.0 46.2 %collective-permute-start.44 = (f32[256,256]{1,0:T(8,128)}, f32[256,256]{1,0:T(8,128)}, u32[]{:S(2)}, u32[]{:S(2)}) collective-permute-start(f32[256,256]{1,0:T(8,128)} %get-tuple-element.166), channel_id=1, source_target_pairs={{1,3},{49,51},{97,99},{145,147},{193,195},{241,243},{289,291},{337... | collective-permute-start | bytes 786440 | tf_op jit(solution)/shard_map/ppermute | solution.py:53
  392.3 30.5 %collective-permute-start.46 = (f32[256,256]{1,0:T(8,128)}, f32[256,256]{1,0:T(8,128)S(1)}, u32[]{:S(2)}, u32[]{:S(2)}) collective-permute-start(f32[256,256]{1,0:T(8,128)} %copy-done.6), channel_id=1, source_target_pairs={{1,2},{49,50},{97,98},{145,146},{193,194},{241,242},{289,290},{337... | collective-permute-start | bytes 786440 | tf_op jit(solution)/shard_map/ppermute | solution.py:53
  393.6 29.9 %collective-permute-start.47 = (f32[256,256]{1,0:T(8,128)}, f32[256,256]{1,0:T(8,128)S(1)}, u32[]{:S(2)}, u32[]{:S(2)}) collective-permute-start(f32[256,256]{1,0:T(8,128)} %copy-done.6), channel_id=1, source_target_pairs={{1,3},{49,51},{97,99},{145,147},{193,195},{241,243},{289,291},{337... | collective-permute-start | bytes 786440 | tf_op jit(solution)/shard_map/ppermute | solution.py:53
  394.3 27.8 %collective-permute-start.45 = (f32[256,256]{1,0:T(8,128)}, f32[256,256]{1,0:T(8,128)S(1)}, u32[]{:S(2)}, u32[]{:S(2)}) collective-permute-start(f32[256,256]{1,0:T(8,128)} %get-tuple-element.166), channel_id=1, source_target_pairs={{3,2},{51,50},{99,98},{147,146},{195,194},{243,242},{291,290},{339... | collective-permute-start | bytes 786440 | tf_op jit(solution)/shard_map/ppermute | solution.py:53
  430.0 3.8 collective-permute-start.30
  431.3 4.5 collective-permute-start.49
  432.0 3.8 collective-permute-start.50
  434.4 33.6 %collective-permute-start.31 = (f32[256,256]{1,0:T(8,128)S(1)}, f32[256,256]{1,0:T(8,128)S(1)}, u32[]{:S(2)}, u32[]{:S(2)}) collective-permute-start(f32[256,256]{1,0:T(8,128)S(1)} %broadcast_select_fusion.2), channel_id=1, source_target_pairs={{98,674},{146,722},{99,675},{147,723},{196,4},{244,52},{197,5},{24... | collective-permute-start | bytes 786440 | tf_op jit(solution)/shard_map/ppermute | solution.py:53
  435.1 32.9 %collective-permute-start.32 = (f32[256,256]{1,0:T(8,128)S(1)}, f32[256,256]{1,0:T(8,128)S(1)}, u32[]{:S(2)}, u32[]{:S(2)}) collective-permute-start(f32[256,256]{1,0:T(8,128)S(1)} %broadcast_select_fusion.2), channel_id=1, source_target_pairs={{98,386},{146,434},{99,387},{147,435},{196,484},{244,532},{197,485... | collective-permute-start | bytes 786440 | tf_op jit(solution)/shard_map/ppermute | solution.py:53
  437.1 54.5 %collective-permute-start.51 = (f32[256,256]{1,0:T(8,128)S(1)}, f32[256,256]{1,0:T(8,128)S(1)}, u32[]{:S(2)}, u32[]{:S(2)}) collective-permute-start(f32[256,256]{1,0:T(8,128)S(1)} %select_select_fusion.4), channel_id=1, source_target_pairs={{98,290},{146,338},{386,578},{434,626},{99,291},{147,339},{387,579... | collective-permute-start | bytes 786440 | tf_op jit(solution)/shard_map/ppermute | solution.py:53
  437.8 53.9 %collective-permute-start.52 = (f32[256,256]{1,0:T(8,128)S(1)}, f32[256,256]{1,0:T(8,128)S(1)}, u32[]{:S(2)}, u32[]{:S(2)}) collective-permute-start(f32[256,256]{1,0:T(8,128)S(1)} %select_select_fusion.4), channel_id=1, source_target_pairs={{98,194},{146,242},{386,482},{434,530},{674,2},{722,50},{99,195},{... | collective-permute-start | bytes 786440 | tf_op jit(solution)/shard_map/ppermute | solution.py:53
  469.3 24.7 %collective-permute-start.33 = (f32[256,256]{1,0:T(8,128)S(1)}, f32[256,256]{1,0:T(8,128)S(1)}, u32[]{:S(2)}, u32[]{:S(2)}) collective-permute-start(f32[256,256]{1,0:T(8,128)S(1)} %select_select_fusion.8), channel_id=1, source_target_pairs={{98,290},{146,338},{386,578},{434,626},{99,291},{147,339},{387,579... | collective-permute-start | bytes 786440 | tf_op jit(solution)/shard_map/ppermute | solution.py:53
  469.9 31.9 %collective-permute-start.34 = (f32[256,256]{1,0:T(8,128)S(1)}, f32[256,256]{1,0:T(8,128)S(1)}, u32[]{:S(2)}, u32[]{:S(2)}) collective-permute-start(f32[256,256]{1,0:T(8,128)S(1)} %select_select_fusion.8), channel_id=1, source_target_pairs={{98,194},{146,242},{386,482},{434,530},{674,2},{722,50},{99,195},{... | collective-permute-start | bytes 786440 | tf_op jit(solution)/shard_map/ppermute | solution.py:53
  (43 other events, 1022.7 us)
where the time goes:
time: 516 us; the launch traced here: 506 us
  starting transfers between devices  223 us (43%)
  waiting for transfers between devices  189 us (37%)
  local copies, waits for them, and re-layouts  46.8 us (9%)
  other arithmetic  35.1 us (7%)
  matrix products  9.48 us (2%)
    ppermute x53, starting transfers between devices, send(): got = lax.ppermute(value, AXES, perm)  223 us
    ppermute x53, waiting for transfers between devices, send(): got = lax.ppermute(value, AXES, perm)  189 us
    dynamic_slice x30, local copies, waits for them, and re-layouts, send(): hit = jnp.asarray(mask)[self.lin]  18.4 us
    select_n x11, other arithmetic, down_columns(): value = jnp.where(hit, got, value)  12.6 us
    select_n x6, other arithmetic, along_rows(): held = jnp.where(hit, got, held)  12.3 us
  transfers between devices with their start and end apart: 53, of which 6 were waited for; matrix products, arithmetic and copies ran while one was open for 14% of the time, Pallas kernels for 0%

commit v1 on v0

--- a/solution.py
+++ b/solution.py
@@ -56,8 +56,9 @@
         hit = jnp.asarray(mask)[self.lin]
         return got, hit
 
-    def down_columns(self, value, roots):
+    def plan_down(self, roots):
         ny, nk, nz, nx = self.shape
+        rounds = []
         pairs = []
         for c, r in roots.items():
             z, x = divmod(c, nx)
@@ -66,10 +67,9 @@
                 if k != k0:
                     pairs.append(((y0, k0, z, x), (y0, k, z, x)))
         if pairs:
-            got, hit = self.send(value, pairs)
-            value = jnp.where(hit, got, value)
+            rounds.append([pairs])
         for sends in split_rounds(ny):
-            results = []
+            level = []
             for offsets in sends:
                 pairs = []
                 for c, r in roots.items():
@@ -78,10 +78,19 @@
                     for a, b in offsets:
                         for k in range(nk):
                             pairs.append((((y0 + a) % ny, k, z, x), ((y0 + b) % ny, k, z, x)))
-                results.append(self.send(value, pairs))
+                level.append(pairs)
+            rounds.append(level)
+        return rounds
+
+    def run(self, value, rounds):
+        for level in rounds:
+            results = [self.send(value, pairs) for pairs in level if pairs]
             for got, hit in results:
                 value = jnp.where(hit, got, value)
         return value
+
+    def down_columns(self, value, roots):
+        return self.run(value, self.plan_down(roots))
 
     def along_rows(self, tiles, root_col, skip=()):
         ny, nk, nz, nx = self.shape
@@ -160,21 +169,20 @@
         return jnp.where(is_root, tiles, out)
 
 
-def solve_panel(factor, blocks):
-    count = blocks.shape[0]
-    width = blocks.shape[-1]
-    stacked = jnp.transpose(blocks, (2, 0, 1)).reshape(width, count * width)
-    solved = jax.scipy.linalg.solve_triangular(factor, stacked, lower=True)
-    return jnp.transpose(solved.reshape(width, count, width), (1, 2, 0))
-
-
 def products(rows, far):
     return jnp.einsum("sab,db->sad", rows, far, precision=lax.Precision.HIGHEST)
+
+
+def factor_and_inverse(tile):
+    factor = jnp.linalg.cholesky(tile)
+    eye = jnp.eye(tile.shape[-1], dtype=tile.dtype)
+    return factor, jax.scipy.linalg.solve_triangular(factor, eye, lower=True)
 
 
 def make_on_device(shape):
     def on_device(matrix, present, update):
         g = Grid(shape)
+        ny, nk, nz, nx = shape
         tiles = matrix[:, 0, 0]
         listed = present[:, 0, 0].astype(jnp.float32)
         flags = update[:, :, 0, 0].astype(jnp.float32)
@@ -183,26 +191,33 @@
         identity = jnp.eye(width, dtype=jnp.float32)
         far_slot = g.col // n_row
         far_root = {c: c % n_row for c in range(2, n_col)}
-
-        def factor_on_owner(k, tile):
-            owner = (g.row == k) & (g.col == k)
-            factor = lax.cond(owner, jnp.linalg.cholesky, lambda t: identity, tile)
-            return owner, g.down_columns(factor, {k: k})
-
-        def solve_column(k, owner, factor, work):
-            solved = lax.cond(g.col == k, lambda d: solve_panel(factor, d), lambda d: d, work)
-            return solved.at[0].set(jnp.where(owner, factor, solved[0]))
-
-        owner0, factor0 = factor_on_owner(0, tiles[0])
-        p0 = solve_column(0, owner0, factor0, tiles)
-        got, _ = g.send(p0[0], [((0, 1, 0, 0), (0, 1, 0, 1))])
-        work11 = tiles[0] - flags[0, 0] * products(got[None], got)[0]
-        f01 = g.down_columns(p0[0], {0: 1 % n_row})
-        pairs = [((y, k, 0, 0), (y, k, 0, 1)) for y in range(shape[0]) for k in range(shape[1])]
-        q01, _ = g.send(products(p0, f01), pairs)
-        owner1, factor1 = factor_on_owner(1, work11)
-        work1 = tiles - flags[0][:, None, None] * q01
-        p1 = solve_column(1, owner1, factor1, work1)
+        rows = [(y, k) for y in range(ny) for k in range(nk)]
+        owner0 = (g.row == 0) & (g.col == 0)
+        owner1 = (g.row == 1) & (g.col == 1)
+
+        a_row0, _ = g.send(tiles, [((y, k, 0, 0), (y, k, 0, 1)) for y, k in rows])
+        a10, _ = g.send(tiles[0], [((0, 1, 0, 0), (0, 1, 0, 1))])
+        a10 = g.down_columns(a10, {1: 1})
+
+        factor0, inverse0 = lax.cond(owner0, factor_and_inverse, lambda t: (identity, identity), tiles[0])
+        first = g.plan_down({0: 0})
+        second = g.plan_down({1: 0})
+        joint = [first[0] + [[((0, 0, 0, 0), (0, 0, 0, 1))]]]
+        for level in range(1, max(len(first), len(second) + 1)):
+            here = first[level] if level < len(first) else []
+            there = second[level - 1] if level - 1 < len(second) else []
+            merged = [a + b for a, b in zip(here, there)] + here[len(there):] + there[len(here):]
+            joint.append(merged)
+        inverse0 = g.run(inverse0, joint)
+        source0 = jnp.where(g.col == 1, a_row0, tiles)
+        p0 = lax.cond((g.col == 0) | (g.col == 1), lambda d: products(d, inverse0), lambda d: d, source0)
+        far01 = products(a10[None], inverse0)[0]
+        work1 = tiles - flags[0][:, None, None] * products(p0, far01)
+        factor1, inverse1 = lax.cond(owner1, factor_and_inverse, lambda t: (identity, identity), work1[0])
+        inverse1 = g.down_columns(inverse1, {1: 1})
+        p1 = lax.cond(g.col == 1, lambda d: products(d, inverse1), lambda d: d, work1)
+        p1 = p1.at[0].set(jnp.where(owner1, factor1, p1[0]))
+        p0 = p0.at[0].set(jnp.where(owner0, factor0, p0[0]))
 
         r0 = g.along_rows(p0, 0, skip=(1,))
         f0 = g.down_columns(lax.dynamic_index_in_dim(r0, far_slot, 0, keepdims=False), far_root)

time: 516 us -> 552 us (1.070)
  starting transfers between devices: 223 us -> 338 us
  waiting for transfers between devices: 189 us -> 100 us
  loops' own time: 0.74 us -> 12.2 us
    ppermute x53 -> x56, starting transfers between devices: 223 us -> 338 us  [send(): got = lax.ppermute(value, AXES, perm)]
    ppermute x53 -> x56, waiting for transfers between devices: 189 us -> 100 us  [send(): got = lax.ppermute(value, AXES, perm)]
    another operation x4, loops' own time: 0.74 us -> 12.2 us  [the longest x1 7.45 us: on_device(): lax.cond(owner1, factor_and_inverse, lambda t: (identity, identity), work...]
    select_n x11 -> x14, other arithmetic: 12.6 us -> 17.4 us  [the longest x12 16.5 us: run(): value = jnp.where(hit, got, value)]
    unnamed x85 -> x88, local copies, waits for them, and re-layouts: 8.71 us -> 11.4 us
    dynamic_slice x30 -> x29, local copies, waits for them, and re-layouts: 18.4 us -> 18 us  [send(): hit = jnp.asarray(mask)[self.lin]]
  transfers between devices with their start and end apart: 53 -> 56, of which waited for: 6 -> 6; matrix products, arithmetic and copies ran while one was open for 14% -> 13% of each run, Pallas kernels for 0% -> 0%
where the time goes in v1:
time: 552 us; the launch traced here: 542 us
  starting transfers between devices  338 us (61%)
  waiting for transfers between devices  100 us (18%)
  local copies, waits for them, and re-layouts  44.3 us (8%)
  other arithmetic  36.8 us (7%)
  loops' own time  12.2 us (2%)
  matrix products  9.26 us (2%)
    ppermute x56, starting transfers between devices, send(): got = lax.ppermute(value, AXES, perm)  338 us
    ppermute x56, waiting for transfers between devices, send(): got = lax.ppermute(value, AXES, perm)  100 us
    dynamic_slice x29, local copies, waits for them, and re-layouts, send(): hit = jnp.asarray(mask)[self.lin]  18 us
    select_n x12, other arithmetic, run(): value = jnp.where(hit, got, value)  16.5 us
    select_n x6, other arithmetic, along_rows(): held = jnp.where(hit, got, held)  12.3 us
    unnamed x88, local copies, waits for them, and re-layouts  11.4 us
  transfers between devices with their start and end apart: 56, of which 6 were waited for; matrix products, arithmetic and copies ran while one was open for 13% of the time, Pallas kernels for 0%

profile of v1, /device:TPU:4, one launch (start us, length us, event | category | flops | bytes accessed | tf_op | source)
XLA Modules:
  0.0 541.9 jit_solution(5418646656318022941)
XLA Ops:
  1.1 4.7 conditional.4
  7.4 1.4 collective-permute-start.9
  15.6 1.4 select_select_fusion.16
  19.8 1.6 broadcast_select_fusion.7
  29.0 2.0 select_select_fusion.13
  36.9 2.6 convolution_bitcast_fusion.1
  42.7 8.2 %conditional.6 = (f32[256,256]{1,0:T(8,128)S(1)}, f32[256,256]{1,0:T(8,128)}) conditional(s32[]{:T(128)} %convert_element_type.44, (f32[256,256]{1,0:T(8,128)S(1)}, f32[256,256]{1,0:T(8,128)S(1)}) %tuple.77, f32[4,256,256]{1,2,0:T(8,128)} %copy.54), branch_computations={%region_8.11_spmd, %region_9.12_spmd} | conditional | flops 202096896 | bytes 8522035 | solution.py:216
  54.6 1.6 broadcast_select_fusion.6
  59.5 78.8 %collective-permute-done.21 = f32[256,256]{1,0:T(8,128)S(1)} collective-permute-done((f32[256,256]{1,0:T(8,128)S(1)}, f32[256,256]{1,0:T(8,128)S(1)}, u32[]{:S(2)}, u32[]{:S(2)}) %collective-permute-start.21) | collective-permute-done | bytes 262176 | tf_op jit(solution)/shard_map/ppermute | solution.py:53
  138.2 2.6 select_select_fusion.11
  140.8 2.0 collective-permute-start.23
  142.8 2.0 collective-permute-start.24
  144.8 2.0 select_select_fusion.12
  151.5 3.0 select_select_fusion.10
  154.5 82.9 %collective-permute-start.25 = (f32[256,256]{1,0:T(8,128)}, f32[256,256]{1,0:T(8,128)}, u32[]{:S(2)}, u32[]{:S(2)}) collective-permute-start(f32[256,256]{1,0:T(8,128)} %select_select_fusion.10), channel_id=1, source_target_pairs={{0,12},{48,60},{96,108},{144,156},{192,204},{240,252},{288,300},{3... | collective-permute-start | bytes 786440 | tf_op jit(solution)/shard_map/ppermute | solution.py:53
  237.5 5.3 collective-permute-start.26
  244.6 1.6 copy.56
  252.7 2.3 select_select_fusion.9
  256.3 4.4 collective-permute-done.40
  260.7 1.9 select_select_fusion.7
  262.7 4.8 collective-permute-start.41
  271.5 1.5 bitcast_dynamic-update-slice_fusion.13
  273.0 10.6 %collective-permute-start.28 = (f32[256,256]{1,0:T(8,128)}, f32[256,256]{1,0:T(8,128)}, u32[]{:S(2)}, u32[]{:S(2)}) collective-permute-start(f32[256,256]{1,0:T(8,128)} %get-tuple-element.210), channel_id=1, source_target_pairs={{2,3},{50,51},{98,99},{146,147},{194,195},{242,243},{290,291},{338... | collective-permute-start | bytes 786440 | tf_op jit(solution)/shard_map/ppermute | solution.py:53
  284.9 20.5 %collective-permute-start.43 = (f32[256,256]{1,0:T(8,128)S(1)}, f32[256,256]{1,0:T(8,128)}, u32[]{:S(2)}, u32[]{:S(2)}) collective-permute-start(f32[256,256]{1,0:T(8,128)S(1)} %select_select_fusion.6), channel_id=1, source_target_pairs={{4,16},{52,64},{100,112},{148,160},{196,208},{244,256},{292,304},{... | collective-permute-start | bytes 786440 | tf_op jit(solution)/shard_map/ppermute | solution.py:53
  305.4 20.3 %collective-permute-start.44 = (f32[256,256]{1,0:T(8,128)S(1)}, f32[256,256]{1,0:T(8,128)}, u32[]{:S(2)}, u32[]{:S(2)}) collective-permute-start(f32[256,256]{1,0:T(8,128)S(1)} %select_select_fusion.6), channel_id=1, source_target_pairs={{4,12},{52,60},{100,108},{148,156},{196,204},{244,252},{292,300},{... | collective-permute-start | bytes 786440 | tf_op jit(solution)/shard_map/ppermute | solution.py:53
  330.0 18.6 %collective-permute-start.29 = (f32[256,256]{1,0:T(8,128)}, f32[256,256]{1,0:T(8,128)S(1)}, u32[]{:S(2)}, u32[]{:S(2)}) collective-permute-start(f32[256,256]{1,0:T(8,128)} %get-tuple-element.210), channel_id=1, source_target_pairs={{0,2},{48,50},{96,98},{144,146},{192,194},{240,242},{288,290},{336... | collective-permute-start | bytes 786440 | tf_op jit(solution)/shard_map/ppermute | solution.py:53
  348.6 1.7 bitcast_dynamic-update-slice_fusion.12
  351.6 20.5 %collective-permute-start.30 = (f32[256,256]{1,0:T(8,128)}, f32[256,256]{1,0:T(8,128)S(1)}, u32[]{:S(2)}, u32[]{:S(2)}) collective-permute-start(f32[256,256]{1,0:T(8,128)} %get-tuple-element.210), channel_id=1, source_target_pairs={{0,3},{48,51},{96,99},{144,147},{192,195},{240,243},{288,291},{336... | collective-permute-start | bytes 786440 | tf_op jit(solution)/shard_map/ppermute | solution.py:53
  373.3 4.5 collective-permute-start.45
  378.5 2.2 collective-permute-done.30
  382.1 1.5 collective-permute-done.45
  383.6 1.4 bitcast_dynamic-update-slice_fusion.7
  385.1 19.1 %collective-permute-start.46 = (f32[256,256]{1,0:T(8,128)}, f32[256,256]{1,0:T(8,128)}, u32[]{:S(2)}, u32[]{:S(2)}) collective-permute-start(f32[256,256]{1,0:T(8,128)} %get-tuple-element.214), channel_id=1, source_target_pairs={{1,2},{49,50},{97,98},{145,146},{193,194},{241,242},{289,290},{337... | collective-permute-start | bytes 786440 | tf_op jit(solution)/shard_map/ppermute | solution.py:53
  404.9 20.5 %collective-permute-start.47 = (f32[256,256]{1,0:T(8,128)}, f32[256,256]{1,0:T(8,128)}, u32[]{:S(2)}, u32[]{:S(2)}) collective-permute-start(f32[256,256]{1,0:T(8,128)} %get-tuple-element.214), channel_id=1, source_target_pairs={{1,3},{49,51},{97,99},{145,147},{193,195},{241,243},{289,291},{337... | collective-permute-start | bytes 786440 | tf_op jit(solution)/shard_map/ppermute | solution.py:53
  426.2 3.0 gather_fusion
  429.2 19.8 %collective-permute-start.48 = (f32[256,256]{1,0:T(8,128)}, f32[256,256]{1,0:T(8,128)S(1)}, u32[]{:S(2)}, u32[]{:S(2)}) collective-permute-start(f32[256,256]{1,0:T(8,128)} %get-tuple-element.214), channel_id=1, source_target_pairs={{3,2},{51,50},{99,98},{147,146},{195,194},{243,242},{291,290},{339... | collective-permute-start | bytes 786440 | tf_op jit(solution)/shard_map/ppermute | solution.py:53
  449.0 1.7 bitcast_dynamic-update-slice_fusion.6
  450.7 1.7 bitcast_dynamic-update-slice_fusion.5
  452.4 5.3 collective-permute-done.48
  458.3 1.7 bitcast_dynamic-update-slice_fusion.3
  460.7 3.0 gather_fusion.1
  463.7 1.5 select_select_fusion.2
  472.3 1.4 select_select_fusion.4
  474.4 28.6 %collective-permute-start.55 = (f32[256,256]{1,0:T(8,128)S(1)}, f32[256,256]{1,0:T(8,128)S(1)}, u32[]{:S(2)}, u32[]{:S(2)}) collective-permute-start(f32[256,256]{1,0:T(8,128)S(1)} %select_select_fusion.4), channel_id=1, source_target_pairs={{98,194},{146,242},{386,482},{434,530},{674,2},{722,50},{99,195},{... | collective-permute-start | bytes 786440 | tf_op jit(solution)/shard_map/ppermute | solution.py:53
  506.3 21.7 %collective-permute-start.37 = (f32[256,256]{1,0:T(8,128)S(1)}, f32[256,256]{1,0:T(8,128)S(1)}, u32[]{:S(2)}, u32[]{:S(2)}) collective-permute-start(f32[256,256]{1,0:T(8,128)S(1)} %select_select_fusion.8), channel_id=1, source_target_pairs={{98,194},{146,242},{386,482},{434,530},{674,2},{722,50},{99,195},{... | collective-permute-start | bytes 786440 | tf_op jit(solution)/shard_map/ppermute | solution.py:53
  528.0 2.3 convolution_multiply_fusion
  530.3 8.0 %collective-permute-done.37 = f32[256,256]{1,0:T(8,128)S(1)} collective-permute-done((f32[256,256]{1,0:T(8,128)S(1)}, f32[256,256]{1,0:T(8,128)S(1)}, u32[]{:S(2)}, u32[]{:S(2)}) %collective-permute-start.37) | collective-permute-done | bytes 262176 | tf_op jit(solution)/shard_map/ppermute | solution.py:53
  538.3 3.4 fusion.32
  (239 shorter events, 79.6 us)
Async XLA Ops:
  7.4 5.4 %collective-permute-start.9 = (f32[256,256]{1,0:T(8,128)S(1)}, f32[256,256]{1,0:T(8,128)}, u32[]{:S(2)}, u32[]{:S(2)}) collective-permute-start(f32[256,256]{1,0:T(8,128)S(1)} %slice_bitcast_fusion.18), channel_id=1, source_target_pairs={{48,49}} | collective-permute-start | bytes 786440 | tf_op jit(solution)/shard_map/ppermute | solution.py:53
  12.9 6.9 %collective-permute-start.10 = (f32[256,256]{1,0:T(8,128)}, f32[256,256]{1,0:T(8,128)S(1)}, u32[]{:S(2)}, u32[]{:S(2)}) collective-permute-start(f32[256,256]{1,0:T(8,128)} %collective-permute-done.9), channel_id=1, source_target_pairs={{49,1}} | collective-permute-start | bytes 786440 | tf_op jit(solution)/shard_map/ppermute | solution.py:53
  13.6 20.2 %collective-permute-start = (f32[4,256,256]{2,1,0:T(8,128)S(1)}, f32[4,256,256]{2,1,0:T(8,128)S(1)}, u32[]{:S(2)}, u32[]{:S(2)}) collective-permute-start(f32[4,256,256]{2,1,0:T(8,128)S(1)} %bitcast.201), channel_id=1, source_target_pairs={{0,1},{48,49},{96,97},{144,145},{192,193},{240,241},{288,289},{336... | collective-permute-start | bytes 3145736 | tf_op jit(solution)/shard_map/ppermute | solution.py:53
  17.0 9.4 %collective-permute-start.5 = (f32[256,256]{1,0:T(8,128)S(1)}, f32[256,256]{1,0:T(8,128)}, u32[]{:S(2)}, u32[]{:S(2)}) collective-permute-start(f32[256,256]{1,0:T(8,128)S(1)} %select_select_fusion.16), channel_id=1, source_target_pairs={{0,192},{48,240},{288,480},{336,528},{1,577},{49,625}} | collective-permute-start | bytes 786440 | tf_op jit(solution)/shard_map/ppermute | solution.py:53
  18.4 8.0 %collective-permute-start.6 = (f32[256,256]{1,0:T(8,128)S(1)}, f32[256,256]{1,0:T(8,128)}, u32[]{:S(2)}, u32[]{:S(2)}) collective-permute-start(f32[256,256]{1,0:T(8,128)S(1)} %select_select_fusion.16), channel_id=1, source_target_pairs={{0,96},{48,144},{288,384},{336,432},{576,672},{624,720},{1,289},{4... | collective-permute-start | bytes 786440 | tf_op jit(solution)/shard_map/ppermute | solution.py:53
  21.4 7.6 %collective-permute-start.11 = (f32[256,256]{1,0:T(8,128)S(1)}, f32[256,256]{1,0:T(8,128)S(1)}, u32[]{:S(2)}, u32[]{:S(2)}) collective-permute-start(f32[256,256]{1,0:T(8,128)S(1)} %broadcast_select_fusion.7), channel_id=1, source_target_pairs={{1,577},{49,625}} | collective-permute-start | bytes 786440 | tf_op jit(solution)/shard_map/ppermute | solution.py:53
  22.1 6.9 %collective-permute-start.12 = (f32[256,256]{1,0:T(8,128)S(1)}, f32[256,256]{1,0:T(8,128)S(1)}, u32[]{:S(2)}, u32[]{:S(2)}) collective-permute-start(f32[256,256]{1,0:T(8,128)S(1)} %broadcast_select_fusion.7), channel_id=1, source_target_pairs={{1,289},{49,337}} | collective-permute-start | bytes 786440 | tf_op jit(solution)/shard_map/ppermute | solution.py:53
  27.6 6.3 %collective-permute-start.7 = (f32[256,256]{1,0:T(8,128)S(1)}, f32[256,256]{1,0:T(8,128)S(1)}, u32[]{:S(2)}, u32[]{:S(2)}) collective-permute-start(f32[256,256]{1,0:T(8,128)S(1)} %select_select_fusion.15), channel_id=1, source_target_pairs={{1,193},{49,241},{289,481},{337,529}} | collective-permute-start | bytes 786440 | tf_op jit(solution)/shard_map/ppermute | solution.py:53
  28.3 5.6 %collective-permute-start.8 = (f32[256,256]{1,0:T(8,128)S(1)}, f32[256,256]{1,0:T(8,128)S(1)}, u32[]{:S(2)}, u32[]{:S(2)}) collective-permute-start(f32[256,256]{1,0:T(8,128)S(1)} %select_select_fusion.15), channel_id=1, source_target_pairs={{1,97},{49,145},{289,385},{337,433},{577,673},{625,721}} | collective-permute-start | bytes 786440 | tf_op jit(solution)/shard_map/ppermute | solution.py:53
  31.0 5.8 %collective-permute-start.13 = (f32[256,256]{1,0:T(8,128)}, f32[256,256]{1,0:T(8,128)}, u32[]{:S(2)}, u32[]{:S(2)}) collective-permute-start(f32[256,256]{1,0:T(8,128)} %select_select_fusion.13), channel_id=1, source_target_pairs={{1,193},{49,241},{289,481},{337,529}} | collective-permute-start | bytes 786440 | tf_op jit(solution)/shard_map/ppermute | solution.py:53
  32.4 4.5 collective-permute-start.14
  51.9 7.6 %collective-permute-start.20 = (f32[256,256]{1,0:T(8,128)S(1)}, f32[256,256]{1,0:T(8,128)S(1)}, u32[]{:S(2)}, u32[]{:S(2)}) collective-permute-start(f32[256,256]{1,0:T(8,128)S(1)} %get-tuple-element.237), channel_id=1, source_target_pairs={{0,3},{48,51},{96,99},{144,147},{192,195},{240,243},{288,291},{336... | collective-permute-start | bytes 786440 | tf_op jit(solution)/shard_map/ppermute | solution.py:53
  52.5 85.7 %collective-permute-start.21 = (f32[256,256]{1,0:T(8,128)S(1)}, f32[256,256]{1,0:T(8,128)S(1)}, u32[]{:S(2)}, u32[]{:S(2)}) collective-permute-start(f32[256,256]{1,0:T(8,128)S(1)} %get-tuple-element.236), channel_id=1, source_target_pairs={{0,2},{48,50},{96,98},{144,146},{192,194},{240,242},{288,290},{336... | collective-permute-start | bytes 786440 | tf_op jit(solution)/shard_map/ppermute | solution.py:53
  53.9 84.4 %collective-permute-start.22 = (f32[256,256]{1,0:T(8,128)S(1)}, f32[256,256]{1,0:T(8,128)S(1)}, u32[]{:S(2)}, u32[]{:S(2)}) collective-permute-start(f32[256,256]{1,0:T(8,128)S(1)} %get-tuple-element.235), channel_id=1, source_target_pairs={{0,5},{48,53},{96,101},{144,149},{192,197},{240,245},{288,293},{33... | collective-permute-start | bytes 786440 | tf_op jit(solution)/shard_map/ppermute | solution.py:53
  56.2 88.6 %collective-permute-start.16 = (f32[256,256]{1,0:T(8,128)S(1)}, f32[256,256]{1,0:T(8,128)S(1)}, u32[]{:S(2)}, u32[]{:S(2)}) collective-permute-start(f32[256,256]{1,0:T(8,128)S(1)} %broadcast_select_fusion.6), channel_id=1, source_target_pairs={{1,577},{49,625}} | collective-permute-start | bytes 786440 | tf_op jit(solution)/shard_map/ppermute | solution.py:53
  56.9 88.0 %collective-permute-start.17 = (f32[256,256]{1,0:T(8,128)S(1)}, f32[256,256]{1,0:T(8,128)S(1)}, u32[]{:S(2)}, u32[]{:S(2)}) collective-permute-start(f32[256,256]{1,0:T(8,128)S(1)} %broadcast_select_fusion.6), channel_id=1, source_target_pairs={{1,289},{49,337}} | collective-permute-start | bytes 786440 | tf_op jit(solution)/shard_map/ppermute | solution.py:53
  140.8 10.7 %collective-permute-start.23 = (f32[256,256]{1,0:T(8,128)}, f32[256,256]{1,0:T(8,128)}, u32[]{:S(2)}, u32[]{:S(2)}) collective-permute-start(f32[256,256]{1,0:T(8,128)} %select_select_fusion.11), channel_id=1, source_target_pairs={{0,32},{48,80},{96,128},{144,176},{192,224},{240,272},{288,320},{3... | collective-permute-start | bytes 786440 | tf_op jit(solution)/shard_map/ppermute | solution.py:53
  142.8 8.7 %collective-permute-start.24 = (f32[256,256]{1,0:T(8,128)}, f32[256,256]{1,0:T(8,128)}, u32[]{:S(2)}, u32[]{:S(2)}) collective-permute-start(f32[256,256]{1,0:T(8,128)} %select_select_fusion.11), channel_id=1, source_target_pairs={{0,16},{48,64},{96,112},{144,160},{192,208},{240,256},{288,304},{3... | collective-permute-start | bytes 786440 | tf_op jit(solution)/shard_map/ppermute | solution.py:53
  146.8 95.9 %collective-permute-start.18 = (f32[256,256]{1,0:T(8,128)}, f32[256,256]{1,0:T(8,128)}, u32[]{:S(2)}, u32[]{:S(2)}) collective-permute-start(f32[256,256]{1,0:T(8,128)} %select_select_fusion.12), channel_id=1, source_target_pairs={{1,97},{49,145},{289,385},{337,433},{577,673},{625,721}} | collective-permute-start | bytes 786440 | tf_op jit(solution)/shard_map/ppermute | solution.py:53
  148.2 94.6 %collective-permute-start.19 = (f32[256,256]{1,0:T(8,128)}, f32[256,256]{1,0:T(8,128)}, u32[]{:S(2)}, u32[]{:S(2)}) collective-permute-start(f32[256,256]{1,0:T(8,128)} %select_select_fusion.12), channel_id=1, source_target_pairs={{1,193},{49,241},{289,481},{337,529}} | collective-permute-start | bytes 786440 | tf_op jit(solution)/shard_map/ppermute | solution.py:53
  154.5 98.2 %collective-permute-start.25 = (f32[256,256]{1,0:T(8,128)}, f32[256,256]{1,0:T(8,128)}, u32[]{:S(2)}, u32[]{:S(2)}) collective-permute-start(f32[256,256]{1,0:T(8,128)} %select_select_fusion.10), channel_id=1, source_target_pairs={{0,12},{48,60},{96,108},{144,156},{192,204},{240,252},{288,300},{3... | collective-permute-start | bytes 786440 | tf_op jit(solution)/shard_map/ppermute | solution.py:53
  237.5 15.3 %collective-permute-start.26 = (f32[256,256]{1,0:T(8,128)}, f32[256,256]{1,0:T(8,128)}, u32[]{:S(2)}, u32[]{:S(2)}) collective-permute-start(f32[256,256]{1,0:T(8,128)} %select_select_fusion.10), channel_id=1, source_target_pairs={{0,8},{48,56},{96,104},{144,152},{192,200},{240,248},{288,296},{33... | collective-permute-start | bytes 786440 | tf_op jit(solution)/shard_map/ppermute | solution.py:53
  248.0 8.3 %collective-permute-start.38 = (f32[256,256]{1,0:T(8,128)}, f32[256,256]{1,0:T(8,128)S(1)}, u32[]{:S(2)}, u32[]{:S(2)}) collective-permute-start(f32[256,256]{1,0:T(8,128)} %get-tuple-element.240), channel_id=1, source_target_pairs={{1,4},{49,52},{97,100},{145,148},{193,196},{241,244},{289,292},{33... | collective-permute-start | bytes 786440 | tf_op jit(solution)/shard_map/ppermute | solution.py:53
  248.8 7.5 %collective-permute-start.39 = (f32[256,256]{1,0:T(8,128)S(1)}, f32[256,256]{1,0:T(8,128)S(1)}, u32[]{:S(2)}, u32[]{:S(2)}) collective-permute-start(f32[256,256]{1,0:T(8,128)S(1)} %get-tuple-element.239), channel_id=1, source_target_pairs={{1,3},{49,51},{97,99},{145,147},{193,195},{241,243},{289,291},{337... | collective-permute-start | bytes 786440 | tf_op jit(solution)/shard_map/ppermute | solution.py:53
  249.5 11.2 %collective-permute-start.40 = (f32[256,256]{1,0:T(8,128)S(1)}, f32[256,256]{1,0:T(8,128)S(1)}, u32[]{:S(2)}, u32[]{:S(2)}) collective-permute-start(f32[256,256]{1,0:T(8,128)S(1)} %get-tuple-element.238), channel_id=1, source_target_pairs={{1,2},{49,50},{97,98},{145,146},{193,194},{241,242},{289,290},{337... | collective-permute-start | bytes 786440 | tf_op jit(solution)/shard_map/ppermute | solution.py:53
  255.0 16.5 %collective-permute-start.27 = (f32[256,256]{1,0:T(8,128)S(1)}, f32[256,256]{1,0:T(8,128)S(1)}, u32[]{:S(2)}, u32[]{:S(2)}) collective-permute-start(f32[256,256]{1,0:T(8,128)S(1)} %select_select_fusion.9), channel_id=1, source_target_pairs={{0,4},{48,52},{96,100},{144,148},{192,196},{240,244},{288,292},{33... | collective-permute-start | bytes 786440 | tf_op jit(solution)/shard_map/ppermute | solution.py:53
  262.7 20.9 %collective-permute-start.41 = (f32[256,256]{1,0:T(8,128)S(1)}, f32[256,256]{1,0:T(8,128)S(1)}, u32[]{:S(2)}, u32[]{:S(2)}) collective-permute-start(f32[256,256]{1,0:T(8,128)S(1)} %select_select_fusion.7), channel_id=1, source_target_pairs={{4,36},{52,84},{100,132},{148,180},{196,228},{244,276},{292,324},{... | collective-permute-start | bytes 786440 | tf_op jit(solution)/shard_map/ppermute | solution.py:53
  267.5 16.0 %collective-permute-start.42 = (f32[256,256]{1,0:T(8,128)S(1)}, f32[256,256]{1,0:T(8,128)S(1)}, u32[]{:S(2)}, u32[]{:S(2)}) collective-permute-start(f32[256,256]{1,0:T(8,128)S(1)} %select_select_fusion.7), channel_id=1, source_target_pairs={{4,20},{52,68},{100,116},{148,164},{196,212},{244,260},{292,308},{... | collective-permute-start | bytes 786440 | tf_op jit(solution)/shard_map/ppermute | solution.py:53
  273.0 57.0 %collective-permute-start.28 = (f32[256,256]{1,0:T(8,128)}, f32[256,256]{1,0:T(8,128)}, u32[]{:S(2)}, u32[]{:S(2)}) collective-permute-start(f32[256,256]{1,0:T(8,128)} %get-tuple-element.210), channel_id=1, source_target_pairs={{2,3},{50,51},{98,99},{146,147},{194,195},{242,243},{290,291},{338... | collective-permute-start | bytes 786440 | tf_op jit(solution)/shard_map/ppermute | solution.py:53
  284.9 65.4 %collective-permute-start.43 = (f32[256,256]{1,0:T(8,128)S(1)}, f32[256,256]{1,0:T(8,128)}, u32[]{:S(2)}, u32[]{:S(2)}) collective-permute-start(f32[256,256]{1,0:T(8,128)S(1)} %select_select_fusion.6), channel_id=1, source_target_pairs={{4,16},{52,64},{100,112},{148,160},{196,208},{244,256},{292,304},{... | collective-permute-start | bytes 786440 | tf_op jit(solution)/shard_map/ppermute | solution.py:53
  305.4 46.2 %collective-permute-start.44 = (f32[256,256]{1,0:T(8,128)S(1)}, f32[256,256]{1,0:T(8,128)}, u32[]{:S(2)}, u32[]{:S(2)}) collective-permute-start(f32[256,256]{1,0:T(8,128)S(1)} %select_select_fusion.6), channel_id=1, source_target_pairs={{4,12},{52,60},{100,108},{148,156},{196,204},{244,252},{292,300},{... | collective-permute-start | bytes 786440 | tf_op jit(solution)/shard_map/ppermute | solution.py:53
  328.0 76.2 %collective-permute-start.31 = (f32[256,256]{1,0:T(8,128)}, f32[256,256]{1,0:T(8,128)S(1)}, u32[]{:S(2)}, u32[]{:S(2)}) collective-permute-start(f32[256,256]{1,0:T(8,128)} %copy-done.9), channel_id=1, source_target_pairs={{0,2},{48,50},{96,98},{144,146},{192,194},{240,242},{288,290},{336... | collective-permute-start | bytes 786440 | tf_op jit(solution)/shard_map/ppermute | solution.py:53
  329.3 96.1 %collective-permute-start.32 = (f32[256,256]{1,0:T(8,128)}, f32[256,256]{1,0:T(8,128)S(1)}, u32[]{:S(2)}, u32[]{:S(2)}) collective-permute-start(f32[256,256]{1,0:T(8,128)} %copy-done.9), channel_id=1, source_target_pairs={{0,3},{48,51},{96,99},{144,147},{192,195},{240,243},{288,291},{336... | collective-permute-start | bytes 786440 | tf_op jit(solution)/shard_map/ppermute | solution.py:53
  330.0 43.3 %collective-permute-start.29 = (f32[256,256]{1,0:T(8,128)}, f32[256,256]{1,0:T(8,128)S(1)}, u32[]{:S(2)}, u32[]{:S(2)}) collective-permute-start(f32[256,256]{1,0:T(8,128)} %get-tuple-element.210), channel_id=1, source_target_pairs={{0,2},{48,50},{96,98},{144,146},{192,194},{240,242},{288,290},{336... | collective-permute-start | bytes 786440 | tf_op jit(solution)/shard_map/ppermute | solution.py:53
  350.3 108.1 %collective-permute-start.49 = (f32[256,256]{1,0:T(8,128)}, f32[256,256]{1,0:T(8,128)}, u32[]{:S(2)}, u32[]{:S(2)}) collective-permute-start(f32[256,256]{1,0:T(8,128)} %get-tuple-element.240), channel_id=1, source_target_pairs={{1,2},{49,50},{97,98},{145,146},{193,194},{241,242},{289,290},{337... | collective-permute-start | bytes 786440 | tf_op jit(solution)/shard_map/ppermute | solution.py:53
  351.6 29.1 %collective-permute-start.30 = (f32[256,256]{1,0:T(8,128)}, f32[256,256]{1,0:T(8,128)S(1)}, u32[]{:S(2)}, u32[]{:S(2)}) collective-permute-start(f32[256,256]{1,0:T(8,128)} %get-tuple-element.210), channel_id=1, source_target_pairs={{0,3},{48,51},{96,99},{144,147},{192,195},{240,243},{288,291},{336... | collective-permute-start | bytes 786440 | tf_op jit(solution)/shard_map/ppermute | solution.py:53
  373.3 10.3 %collective-permute-start.45 = (f32[256,256]{1,0:T(8,128)S(1)}, f32[256,256]{1,0:T(8,128)S(1)}, u32[]{:S(2)}, u32[]{:S(2)}) collective-permute-start(f32[256,256]{1,0:T(8,128)S(1)} %select_select_fusion.5), channel_id=1, source_target_pairs={{4,8},{52,56},{100,104},{148,152},{196,200},{244,248},{292,296},{3... | collective-permute-start | bytes 786440 | tf_op jit(solution)/shard_map/ppermute | solution.py:53
  380.7 79.3 %collective-permute-start.50 = (f32[256,256]{1,0:T(8,128)}, f32[256,256]{1,0:T(8,128)S(1)}, u32[]{:S(2)}, u32[]{:S(2)}) collective-permute-start(f32[256,256]{1,0:T(8,128)} %get-tuple-element.240), channel_id=1, source_target_pairs={{1,3},{49,51},{97,99},{145,147},{193,195},{241,243},{289,291},{337... | collective-permute-start | bytes 786440 | tf_op jit(solution)/shard_map/ppermute | solution.py:53
  385.1 63.9 %collective-permute-start.46 = (f32[256,256]{1,0:T(8,128)}, f32[256,256]{1,0:T(8,128)}, u32[]{:S(2)}, u32[]{:S(2)}) collective-permute-start(f32[256,256]{1,0:T(8,128)} %get-tuple-element.214), channel_id=1, source_target_pairs={{1,2},{49,50},{97,98},{145,146},{193,194},{241,242},{289,290},{337... | collective-permute-start | bytes 786440 | tf_op jit(solution)/shard_map/ppermute | solution.py:53
  404.9 45.7 %collective-permute-start.47 = (f32[256,256]{1,0:T(8,128)}, f32[256,256]{1,0:T(8,128)}, u32[]{:S(2)}, u32[]{:S(2)}) collective-permute-start(f32[256,256]{1,0:T(8,128)} %get-tuple-element.214), channel_id=1, source_target_pairs={{1,3},{49,51},{97,99},{145,147},{193,195},{241,243},{289,291},{337... | collective-permute-start | bytes 786440 | tf_op jit(solution)/shard_map/ppermute | solution.py:53
  429.2 28.4 %collective-permute-start.48 = (f32[256,256]{1,0:T(8,128)}, f32[256,256]{1,0:T(8,128)S(1)}, u32[]{:S(2)}, u32[]{:S(2)}) collective-permute-start(f32[256,256]{1,0:T(8,128)} %get-tuple-element.214), channel_id=1, source_target_pairs={{3,2},{51,50},{99,98},{147,146},{195,194},{243,242},{291,290},{339... | collective-permute-start | bytes 786440 | tf_op jit(solution)/shard_map/ppermute | solution.py:53
  467.6 4.7 collective-permute-start.52
  470.9 33.3 %collective-permute-start.34 = (f32[256,256]{1,0:T(8,128)S(1)}, f32[256,256]{1,0:T(8,128)S(1)}, u32[]{:S(2)}, u32[]{:S(2)}) collective-permute-start(f32[256,256]{1,0:T(8,128)S(1)} %broadcast_select_fusion.3), channel_id=1, source_target_pairs={{98,674},{146,722},{99,675},{147,723},{196,4},{244,52},{197,5},{24... | collective-permute-start | bytes 786440 | tf_op jit(solution)/shard_map/ppermute | solution.py:53
  471.6 32.6 %collective-permute-start.35 = (f32[256,256]{1,0:T(8,128)S(1)}, f32[256,256]{1,0:T(8,128)S(1)}, u32[]{:S(2)}, u32[]{:S(2)}) collective-permute-start(f32[256,256]{1,0:T(8,128)S(1)} %broadcast_select_fusion.3), channel_id=1, source_target_pairs={{98,386},{146,434},{99,387},{147,435},{196,484},{244,532},{197,485... | collective-permute-start | bytes 786440 | tf_op jit(solution)/shard_map/ppermute | solution.py:53
  473.7 54.3 %collective-permute-start.54 = (f32[256,256]{1,0:T(8,128)S(1)}, f32[256,256]{1,0:T(8,128)S(1)}, u32[]{:S(2)}, u32[]{:S(2)}) collective-permute-start(f32[256,256]{1,0:T(8,128)S(1)} %select_select_fusion.4), channel_id=1, source_target_pairs={{98,290},{146,338},{386,578},{434,626},{99,291},{147,339},{387,579... | collective-permute-start | bytes 786440 | tf_op jit(solution)/shard_map/ppermute | solution.py:53
  474.4 53.6 %collective-permute-start.55 = (f32[256,256]{1,0:T(8,128)S(1)}, f32[256,256]{1,0:T(8,128)S(1)}, u32[]{:S(2)}, u32[]{:S(2)}) collective-permute-start(f32[256,256]{1,0:T(8,128)S(1)} %select_select_fusion.4), channel_id=1, source_target_pairs={{98,194},{146,242},{386,482},{434,530},{674,2},{722,50},{99,195},{... | collective-permute-start | bytes 786440 | tf_op jit(solution)/shard_map/ppermute | solution.py:53
  505.6 24.6 %collective-permute-start.36 = (f32[256,256]{1,0:T(8,128)S(1)}, f32[256,256]{1,0:T(8,128)S(1)}, u32[]{:S(2)}, u32[]{:S(2)}) collective-permute-start(f32[256,256]{1,0:T(8,128)S(1)} %select_select_fusion.8), channel_id=1, source_target_pairs={{98,290},{146,338},{386,578},{434,626},{99,291},{147,339},{387,579... | collective-permute-start | bytes 786440 | tf_op jit(solution)/shard_map/ppermute | solution.py:53
  506.3 31.9 %collective-permute-start.37 = (f32[256,256]{1,0:T(8,128)S(1)}, f32[256,256]{1,0:T(8,128)S(1)}, u32[]{:S(2)}, u32[]{:S(2)}) collective-permute-start(f32[256,256]{1,0:T(8,128)S(1)} %select_select_fusion.8), channel_id=1, source_target_pairs={{98,194},{146,242},{386,482},{434,530},{674,2},{722,50},{99,195},{... | collective-permute-start | bytes 786440 | tf_op jit(solution)/shard_map/ppermute | solution.py:53
  (48 other events, 1200.9 us)
